TPU v7x, 512 devices: a whole 4x4x16 slice. The times are simulated.
512 devices in a mesh: sect: 8 (over x, y_hi), blk: 64 (over z, y_lo, core).
Axes of the slice: x: 4, y: 4 (y_hi: 2, y_lo: 2; y = y_hi * 2 + y_lo), z: 16, core: 2. Of those that a mesh axis runs over, the one named last changes fastest.
Arguments:
- bits: int32 [8, 1024], P('sect', 'blk'), may hold values from 0 to 1
- labels: int32 [128], replicated, may hold values from 0 to 127, each once
- left: bfloat16 [1024, 16384], P('blk')
- tensors: bfloat16 [8, 2, 128, 128, 128], P('sect', None, 'blk')
Outputs:
- prob: float32 [8, 1024], P('sect', 'blk')
- logprob: float32 [8, 1024], P('sect', 'blk')
Inputs may be any that keep to these rules, and one draw needn't show every extreme that they name: Every charge labels exactly one block.
All inputs are finite; a program needn't handle non-finite values.
Results may differ from a plain program's by a relative error of at most 0.0003.
Values may be sent and summed in bfloat16 or wider, within the bound.
No kernel may reach another device: no remote copies, remote signals or barrier semaphores. Data moves between devices by JAX's collectives and lax.ppermute only.
A program may use at most 64 MiB of HBM per device.

v0:
```python
import jax
import jax.numpy as jnp
from jax import lax
from jax.sharding import PartitionSpec as P


def passed_along(value, axis, steps):
    count = lax.axis_size(axis)
    first, last = (max(0, -steps), min(count, count - steps))
    return lax.ppermute(value, axis, [(source, source + steps) for source in range(first, last)])


def charge_order(labels, left, block):
    count_blocks = labels.shape[0]
    samples_here = left.shape[0]
    blocks = left.reshape(samples_here, count_blocks, block)
    index = jnp.arange(count_blocks, dtype=jnp.int32)
    pick = (labels[None, :] == index[:, None]).astype(jnp.bfloat16)
    ordered = jnp.einsum("ci,rik->rck", pick, blocks, preferred_element_type=jnp.float32)
    return ordered.astype(jnp.bfloat16)


def site_images(state, weights, block):
    count_rows = state.shape[0]
    blocks = state.reshape(count_rows, weights.shape[1], block)
    return jnp.einsum(
        "rck,bckl->brcl",
        blocks,
        weights,
        preferred_element_type=jnp.float32,
        precision=lax.Precision.HIGHEST,
    )


def run_sections(start_rows, site_bits, advance, count):
    segment = lax.axis_index("sect")
    segments = lax.axis_size("sect")
    mrows = start_rows.shape[1]

    def one_step(step, carry):
        state, total, prob_out, log_out = carry
        group = step - segment
        valid = (group >= 0) & (group < count)
        slot = jnp.clip(group, 0, count - 1)
        first = segment == 0
        start_now = lax.dynamic_index_in_dim(start_rows, slot, 0, keepdims=False)
        state = jnp.where(first, start_now, state)
        total = jnp.where(first, jnp.zeros_like(total), total)
        bit_rows = lax.dynamic_index_in_dim(site_bits, slot, 0, keepdims=False)
        prob, next_state = advance(state, bit_rows)
        total = total + jnp.log(prob)
        old_prob = lax.dynamic_index_in_dim(prob_out, slot, 0, keepdims=False)
        old_log = lax.dynamic_index_in_dim(log_out, slot, 0, keepdims=False)
        prob_out = lax.dynamic_update_index_in_dim(
            prob_out, jnp.where(valid, prob, old_prob), slot, 0
        )
        log_out = lax.dynamic_update_index_in_dim(
            log_out, jnp.where(valid, total, old_log), slot, 0
        )
        state, total = passed_along((next_state, total), "sect", 1)
        return (state, total, prob_out, log_out)

    empty = jnp.zeros((count, mrows), jnp.float32)
    init = (start_rows[0], jnp.zeros((mrows,), jnp.float32), empty, empty)
    result = lax.fori_loop(0, count + segments - 1, one_step, init)
    return (result[2], result[3])


def body(bits, labels, left, tensors):
    block = tensors.shape[-1]
    count_blocks = labels.shape[0]
    width = count_blocks * block
    rows = bits.shape[1]
    ordered = charge_order(labels, left, block)
    count = 1
    whole = lax.all_gather(tensors, "blk", axis=2, tiled=True)[0]

    def advance(state, bit_rows):
        image = site_images(state, whole, block)
        stay = image[0]
        raised = jnp.roll(image[1], 1, axis=1)
        norm_zero = jnp.sum(stay * stay, axis=(1, 2))
        norm_one = jnp.sum(raised * raised, axis=(1, 2))
        choose = bit_rows == 1
        chosen_norm = jnp.where(choose, norm_one, norm_zero)
        prob = chosen_norm / (norm_zero + norm_one)
        chosen = jnp.where(choose[:, None, None], raised, stay)
        scaled = chosen * lax.rsqrt(chosen_norm / width + 1e-06)[:, None, None]
        return (prob, scaled.reshape(state.shape[0], width))

    mrows = rows // count
    start_rows = ordered.astype(jnp.float32).reshape(count, mrows, width)
    site_bits = bits[0].reshape(count, mrows)
    prob_out, log_out = run_sections(start_rows, site_bits, advance, count)
    return (prob_out, log_out)


def solution(mesh):
    in_specs = (P("sect", "blk"), P(), P("blk", None), P("sect", None, "blk", None, None))
    out_specs = (P("sect", "blk"), P("sect", "blk"))
    return jax.shard_map(body, mesh=mesh, in_specs=in_specs, out_specs=out_specs, check_vma=False)
```

profile of v0, /device:TPU:2, one launch (start us, length us, event | category | flops | bytes accessed | tf_op | source)
XLA Modules:
  0.0 439.7 jit_solution(6856353192765204653)
XLA Ops:
  7.2 1.6 copy.15
  8.8 1.1 copy.22
  10.0 0.9 fusion.7
  10.9 0.6 copy.29
  11.5 1.2 reshape.91
  12.8 130.9 %all-gather.2.cloned.1.call-done = bf16[1,2,128,128,128]{4,3,1,0,2:T(8,128)(2,1)} async-done(((bf16[1,2,2,128,128]{4,3,1,0,2:T(8,128)(2,1)}), bf16[1,2,128,128,128]{4,3,1,0,2:T(8,128)(2,1)}) %all-gather.2.cloned.1.call-update) | async-done | bytes 8388624 | tf_op jit(solution)/shard_map/all_gather | solution.py:76
  143.7 288.7 %while.21 = (s32[]{:T(128)}, f32[16,16384]{1,0:T(8,128)S(1)}, f32[16]{0:T(128)S(1)}, f32[1,16]{1,0:T(1,128)S(1)}, f32[1,16]{1,0:T(1,128)S(1)}, /*index=5*/s32[1,...) while((s32[]{:T(128)}, f32[16,16384]{1,0:T(8,128)S(1)}, ...), condition=%wide.region_3.4_spmd.clone, body=%wide.region_0.3_spmd.clone.sunk | while | flops 807403776 | bytes 34604904 | solution.py:65
  143.7 1.3 fusion.21
  145.2 6.5 %convolution_bitcast_fusion.2 = f32[2,16,128,128]{3,1,0,2:T(8,128)S(1)} fusion(bf16[2,128,128,128]{3,2,0,1:T(8,128)(2,1)} %get-tuple-element.370, f32[16,128,128,1]{2,1,0,3:T(8,128)S(1)} %bitcast.81), kind=kOutput, calls=%fused_computation.clone.1 | convolution fusion | flops 805306368 | bytes 11534336 | tf_op jit(solution)/shard_map/while/body/eval_jaxpr/rck,bckl->brcl/dot_general | solution.py:26
  151.7 0.4 multiply_reduce_fusion.4
  152.8 0.6 fusion.23
  153.4 4.6 %collective-permute-start = (f32[16,16384]{1,0:T(8,128)S(1)}, f32[16,16384]{1,0:T(8,128)S(1)}, u32[]{:S(2)}, u32[]{:S(2)}) collective-permute-start(f32[16,16384]{1,0:T(8,128)S(1)} %fusion.23), channel_id=1, source_target_pairs={{0,64},{64,128},{128,192},{192,256},{256,320},{320,384},{384,448},... | collective-permute-start | bytes 3145736 | tf_op jit(solution)/shard_map/while/body/eval_jaxpr/ppermute | solution.py:10
  158.1 3.6 collective-permute-start.1
  161.7 21.4 %collective-permute-done.1 = f32[16]{0:T(128)S(1)} collective-permute-done((f32[16]{0:T(128)S(1)}, f32[16]{0:T(128)S(1)}, u32[]{:S(2)}, u32[]{:S(2)}) %collective-permute-start.1) | collective-permute-done | bytes 96 | tf_op jit(solution)/shard_map/while/body/eval_jaxpr/ppermute | solution.py:10
  183.1 1.3 fusion.21
  184.7 6.5 %convolution_bitcast_fusion.2 = f32[2,16,128,128]{3,1,0,2:T(8,128)S(1)} fusion(bf16[2,128,128,128]{3,2,0,1:T(8,128)(2,1)} %get-tuple-element.370, f32[16,128,128,1]{2,1,0,3:T(8,128)S(1)} %bitcast.81), kind=kOutput, calls=%fused_computation.clone.1 | convolution fusion | flops 805306368 | bytes 11534336 | tf_op jit(solution)/shard_map/while/body/eval_jaxpr/rck,bckl->brcl/dot_general | solution.py:26
  191.1 0.4 multiply_reduce_fusion.4
  192.3 0.6 fusion.23
  192.9 3.7 collective-permute-start
  196.7 4.5 %collective-permute-start.1 = (f32[16]{0:T(128)S(1)}, f32[16]{0:T(128)S(1)}, u32[]{:S(2)}, u32[]{:S(2)}) collective-permute-start(f32[16]{0:T(128)S(1)} %get-tuple-element.336), channel_id=1, source_target_pairs={{0,64},{64,128},{128,192},{192,256},{256,320},{320,384},{384,448},... | collective-permute-start | bytes 200 | tf_op jit(solution)/shard_map/while/body/eval_jaxpr/ppermute | solution.py:10
  201.2 20.5 %collective-permute-done.1 = f32[16]{0:T(128)S(1)} collective-permute-done((f32[16]{0:T(128)S(1)}, f32[16]{0:T(128)S(1)}, u32[]{:S(2)}, u32[]{:S(2)}) %collective-permute-start.1) | collective-permute-done | bytes 96 | tf_op jit(solution)/shard_map/while/body/eval_jaxpr/ppermute | solution.py:10
  221.7 1.3 fusion.21
  223.2 6.5 %convolution_bitcast_fusion.2 = f32[2,16,128,128]{3,1,0,2:T(8,128)S(1)} fusion(bf16[2,128,128,128]{3,2,0,1:T(8,128)(2,1)} %get-tuple-element.370, f32[16,128,128,1]{2,1,0,3:T(8,128)S(1)} %bitcast.81), kind=kOutput, calls=%fused_computation.clone.1 | convolution fusion | flops 805306368 | bytes 11534336 | tf_op jit(solution)/shard_map/while/body/eval_jaxpr/rck,bckl->brcl/dot_general | solution.py:26
  229.7 0.4 multiply_reduce_fusion.4
  230.8 0.6 fusion.23
  231.5 2.9 collective-permute-start
  234.3 5.4 %collective-permute-start.1 = (f32[16]{0:T(128)S(1)}, f32[16]{0:T(128)S(1)}, u32[]{:S(2)}, u32[]{:S(2)}) collective-permute-start(f32[16]{0:T(128)S(1)} %get-tuple-element.336), channel_id=1, source_target_pairs={{0,64},{64,128},{128,192},{192,256},{256,320},{320,384},{384,448},... | collective-permute-start | bytes 200 | tf_op jit(solution)/shard_map/while/body/eval_jaxpr/ppermute | solution.py:10
  239.8 19.5 %collective-permute-done.1 = f32[16]{0:T(128)S(1)} collective-permute-done((f32[16]{0:T(128)S(1)}, f32[16]{0:T(128)S(1)}, u32[]{:S(2)}, u32[]{:S(2)}) %collective-permute-start.1) | collective-permute-done | bytes 96 | tf_op jit(solution)/shard_map/while/body/eval_jaxpr/ppermute | solution.py:10
  259.3 1.3 fusion.21
  260.8 6.5 %convolution_bitcast_fusion.2 = f32[2,16,128,128]{3,1,0,2:T(8,128)S(1)} fusion(bf16[2,128,128,128]{3,2,0,1:T(8,128)(2,1)} %get-tuple-element.370, f32[16,128,128,1]{2,1,0,3:T(8,128)S(1)} %bitcast.81), kind=kOutput, calls=%fused_computation.clone.1 | convolution fusion | flops 805306368 | bytes 11534336 | tf_op jit(solution)/shard_map/while/body/eval_jaxpr/rck,bckl->brcl/dot_general | solution.py:26
  267.3 0.4 multiply_reduce_fusion.4
  268.4 0.6 fusion.23
  269.1 2.0 collective-permute-start
  271.0 6.3 %collective-permute-start.1 = (f32[16]{0:T(128)S(1)}, f32[16]{0:T(128)S(1)}, u32[]{:S(2)}, u32[]{:S(2)}) collective-permute-start(f32[16]{0:T(128)S(1)} %get-tuple-element.336), channel_id=1, source_target_pairs={{0,64},{64,128},{128,192},{192,256},{256,320},{320,384},{384,448},... | collective-permute-start | bytes 200 | tf_op jit(solution)/shard_map/while/body/eval_jaxpr/ppermute | solution.py:10
  277.3 18.5 %collective-permute-done.1 = f32[16]{0:T(128)S(1)} collective-permute-done((f32[16]{0:T(128)S(1)}, f32[16]{0:T(128)S(1)}, u32[]{:S(2)}, u32[]{:S(2)}) %collective-permute-start.1) | collective-permute-done | bytes 96 | tf_op jit(solution)/shard_map/while/body/eval_jaxpr/ppermute | solution.py:10
  295.9 1.3 fusion.21
  297.4 6.5 %convolution_bitcast_fusion.2 = f32[2,16,128,128]{3,1,0,2:T(8,128)S(1)} fusion(bf16[2,128,128,128]{3,2,0,1:T(8,128)(2,1)} %get-tuple-element.370, f32[16,128,128,1]{2,1,0,3:T(8,128)S(1)} %bitcast.81), kind=kOutput, calls=%fused_computation.clone.1 | convolution fusion | flops 805306368 | bytes 11534336 | tf_op jit(solution)/shard_map/while/body/eval_jaxpr/rck,bckl->brcl/dot_general | solution.py:26
  303.9 0.4 multiply_reduce_fusion.4
  305.0 0.6 fusion.23
  305.7 1.9 collective-permute-start
  307.6 6.3 %collective-permute-start.1 = (f32[16]{0:T(128)S(1)}, f32[16]{0:T(128)S(1)}, u32[]{:S(2)}, u32[]{:S(2)}) collective-permute-start(f32[16]{0:T(128)S(1)} %get-tuple-element.336), channel_id=1, source_target_pairs={{0,64},{64,128},{128,192},{192,256},{256,320},{320,384},{384,448},... | collective-permute-start | bytes 200 | tf_op jit(solution)/shard_map/while/body/eval_jaxpr/ppermute | solution.py:10
  313.9 17.5 %collective-permute-done.1 = f32[16]{0:T(128)S(1)} collective-permute-done((f32[16]{0:T(128)S(1)}, f32[16]{0:T(128)S(1)}, u32[]{:S(2)}, u32[]{:S(2)}) %collective-permute-start.1) | collective-permute-done | bytes 96 | tf_op jit(solution)/shard_map/while/body/eval_jaxpr/ppermute | solution.py:10
  331.5 1.3 fusion.21
  333.0 6.5 %convolution_bitcast_fusion.2 = f32[2,16,128,128]{3,1,0,2:T(8,128)S(1)} fusion(bf16[2,128,128,128]{3,2,0,1:T(8,128)(2,1)} %get-tuple-element.370, f32[16,128,128,1]{2,1,0,3:T(8,128)S(1)} %bitcast.81), kind=kOutput, calls=%fused_computation.clone.1 | convolution fusion | flops 805306368 | bytes 11534336 | tf_op jit(solution)/shard_map/while/body/eval_jaxpr/rck,bckl->brcl/dot_general | solution.py:26
  339.5 0.4 multiply_reduce_fusion.4
  340.6 0.6 fusion.23
  341.3 1.9 collective-permute-start
  343.2 6.3 %collective-permute-start.1 = (f32[16]{0:T(128)S(1)}, f32[16]{0:T(128)S(1)}, u32[]{:S(2)}, u32[]{:S(2)}) collective-permute-start(f32[16]{0:T(128)S(1)} %get-tuple-element.336), channel_id=1, source_target_pairs={{0,64},{64,128},{128,192},{192,256},{256,320},{320,384},{384,448},... | collective-permute-start | bytes 200 | tf_op jit(solution)/shard_map/while/body/eval_jaxpr/ppermute | solution.py:10
  349.6 16.5 %collective-permute-done.1 = f32[16]{0:T(128)S(1)} collective-permute-done((f32[16]{0:T(128)S(1)}, f32[16]{0:T(128)S(1)}, u32[]{:S(2)}, u32[]{:S(2)}) %collective-permute-start.1) | collective-permute-done | bytes 96 | tf_op jit(solution)/shard_map/while/body/eval_jaxpr/ppermute | solution.py:10
  366.1 1.3 fusion.21
  367.6 6.5 %convolution_bitcast_fusion.2 = f32[2,16,128,128]{3,1,0,2:T(8,128)S(1)} fusion(bf16[2,128,128,128]{3,2,0,1:T(8,128)(2,1)} %get-tuple-element.370, f32[16,128,128,1]{2,1,0,3:T(8,128)S(1)} %bitcast.81), kind=kOutput, calls=%fused_computation.clone.1 | convolution fusion | flops 805306368 | bytes 11534336 | tf_op jit(solution)/shard_map/while/body/eval_jaxpr/rck,bckl->brcl/dot_general | solution.py:26
  374.1 0.4 multiply_reduce_fusion.4
  375.2 0.6 fusion.23
  375.9 1.9 collective-permute-start
  377.8 6.3 %collective-permute-start.1 = (f32[16]{0:T(128)S(1)}, f32[16]{0:T(128)S(1)}, u32[]{:S(2)}, u32[]{:S(2)}) collective-permute-start(f32[16]{0:T(128)S(1)} %get-tuple-element.336), channel_id=1, source_target_pairs={{0,64},{64,128},{128,192},{192,256},{256,320},{320,384},{384,448},... | collective-permute-start | bytes 200 | tf_op jit(solution)/shard_map/while/body/eval_jaxpr/ppermute | solution.py:10
  384.2 15.5 %collective-permute-done.1 = f32[16]{0:T(128)S(1)} collective-permute-done((f32[16]{0:T(128)S(1)}, f32[16]{0:T(128)S(1)}, u32[]{:S(2)}, u32[]{:S(2)}) %collective-permute-start.1) | collective-permute-done | bytes 96 | tf_op jit(solution)/shard_map/while/body/eval_jaxpr/ppermute | solution.py:10
  399.7 1.3 fusion.21
  401.3 6.5 %convolution_bitcast_fusion.2 = f32[2,16,128,128]{3,1,0,2:T(8,128)S(1)} fusion(bf16[2,128,128,128]{3,2,0,1:T(8,128)(2,1)} %get-tuple-element.370, f32[16,128,128,1]{2,1,0,3:T(8,128)S(1)} %bitcast.81), kind=kOutput, calls=%fused_computation.clone.1 | convolution fusion | flops 805306368 | bytes 11534336 | tf_op jit(solution)/shard_map/while/body/eval_jaxpr/rck,bckl->brcl/dot_general | solution.py:26
  407.7 0.4 multiply_reduce_fusion.4
  408.9 0.6 fusion.23
  409.5 1.9 collective-permute-start
  411.4 6.3 %collective-permute-start.1 = (f32[16]{0:T(128)S(1)}, f32[16]{0:T(128)S(1)}, u32[]{:S(2)}, u32[]{:S(2)}) collective-permute-start(f32[16]{0:T(128)S(1)} %get-tuple-element.336), channel_id=1, source_target_pairs={{0,64},{64,128},{128,192},{192,256},{256,320},{320,384},{384,448},... | collective-permute-start | bytes 200 | tf_op jit(solution)/shard_map/while/body/eval_jaxpr/ppermute | solution.py:10
  417.8 14.6 %collective-permute-done.1 = f32[16]{0:T(128)S(1)} collective-permute-done((f32[16]{0:T(128)S(1)}, f32[16]{0:T(128)S(1)}, u32[]{:S(2)}, u32[]{:S(2)}) %collective-permute-start.1) | collective-permute-done | bytes 96 | tf_op jit(solution)/shard_map/while/body/eval_jaxpr/ppermute | solution.py:10
  432.4 0.5 copy-done.1
  (96 shorter events, 7.6 us)
Async XLA Ops:
  7.2 136.5 %all-gather.2.cloned.1.call-start = ((), (), s32[]{:S(2)}) async-start(), calls=%async_computation | async-start | bytes 8519680 | tf_op jit(solution)/shard_map/all_gather | solution.py:76
  151.7 0.8 copy-start
  153.4 29.7 %collective-permute-start = (f32[16,16384]{1,0:T(8,128)S(1)}, f32[16,16384]{1,0:T(8,128)S(1)}, u32[]{:S(2)}, u32[]{:S(2)}) collective-permute-start(f32[16,16384]{1,0:T(8,128)S(1)} %fusion.23), channel_id=1, source_target_pairs={{0,64},{64,128},{128,192},{192,256},{256,320},{320,384},{384,448},... | collective-permute-start | bytes 3145736 | tf_op jit(solution)/shard_map/while/body/eval_jaxpr/ppermute | solution.py:10
  158.1 25.0 %collective-permute-start.1 = (f32[16]{0:T(128)S(1)}, f32[16]{0:T(128)S(1)}, u32[]{:S(2)}, u32[]{:S(2)}) collective-permute-start(f32[16]{0:T(128)S(1)} %get-tuple-element.336), channel_id=1, source_target_pairs={{0,64},{64,128},{128,192},{192,256},{256,320},{320,384},{384,448},... | collective-permute-start | bytes 200 | tf_op jit(solution)/shard_map/while/body/eval_jaxpr/ppermute | solution.py:10
  191.1 0.8 copy-start
  192.9 28.8 %collective-permute-start = (f32[16,16384]{1,0:T(8,128)S(1)}, f32[16,16384]{1,0:T(8,128)S(1)}, u32[]{:S(2)}, u32[]{:S(2)}) collective-permute-start(f32[16,16384]{1,0:T(8,128)S(1)} %fusion.23), channel_id=1, source_target_pairs={{0,64},{64,128},{128,192},{192,256},{256,320},{320,384},{384,448},... | collective-permute-start | bytes 3145736 | tf_op jit(solution)/shard_map/while/body/eval_jaxpr/ppermute | solution.py:10
  196.7 25.0 %collective-permute-start.1 = (f32[16]{0:T(128)S(1)}, f32[16]{0:T(128)S(1)}, u32[]{:S(2)}, u32[]{:S(2)}) collective-permute-start(f32[16]{0:T(128)S(1)} %get-tuple-element.336), channel_id=1, source_target_pairs={{0,64},{64,128},{128,192},{192,256},{256,320},{320,384},{384,448},... | collective-permute-start | bytes 200 | tf_op jit(solution)/shard_map/while/body/eval_jaxpr/ppermute | solution.py:10
  229.7 0.8 copy-start
  231.5 27.8 %collective-permute-start = (f32[16,16384]{1,0:T(8,128)S(1)}, f32[16,16384]{1,0:T(8,128)S(1)}, u32[]{:S(2)}, u32[]{:S(2)}) collective-permute-start(f32[16,16384]{1,0:T(8,128)S(1)} %fusion.23), channel_id=1, source_target_pairs={{0,64},{64,128},{128,192},{192,256},{256,320},{320,384},{384,448},... | collective-permute-start | bytes 3145736 | tf_op jit(solution)/shard_map/while/body/eval_jaxpr/ppermute | solution.py:10
  234.3 24.9 %collective-permute-start.1 = (f32[16]{0:T(128)S(1)}, f32[16]{0:T(128)S(1)}, u32[]{:S(2)}, u32[]{:S(2)}) collective-permute-start(f32[16]{0:T(128)S(1)} %get-tuple-element.336), channel_id=1, source_target_pairs={{0,64},{64,128},{128,192},{192,256},{256,320},{320,384},{384,448},... | collective-permute-start | bytes 200 | tf_op jit(solution)/shard_map/while/body/eval_jaxpr/ppermute | solution.py:10
  267.3 0.8 copy-start
  269.1 26.8 %collective-permute-start = (f32[16,16384]{1,0:T(8,128)S(1)}, f32[16,16384]{1,0:T(8,128)S(1)}, u32[]{:S(2)}, u32[]{:S(2)}) collective-permute-start(f32[16,16384]{1,0:T(8,128)S(1)} %fusion.23), channel_id=1, source_target_pairs={{0,64},{64,128},{128,192},{192,256},{256,320},{320,384},{384,448},... | collective-permute-start | bytes 3145736 | tf_op jit(solution)/shard_map/while/body/eval_jaxpr/ppermute | solution.py:10
  271.0 24.8 %collective-permute-start.1 = (f32[16]{0:T(128)S(1)}, f32[16]{0:T(128)S(1)}, u32[]{:S(2)}, u32[]{:S(2)}) collective-permute-start(f32[16]{0:T(128)S(1)} %get-tuple-element.336), channel_id=1, source_target_pairs={{0,64},{64,128},{128,192},{192,256},{256,320},{320,384},{384,448},... | collective-permute-start | bytes 200 | tf_op jit(solution)/shard_map/while/body/eval_jaxpr/ppermute | solution.py:10
  303.9 0.8 copy-start
  305.7 25.8 %collective-permute-start = (f32[16,16384]{1,0:T(8,128)S(1)}, f32[16,16384]{1,0:T(8,128)S(1)}, u32[]{:S(2)}, u32[]{:S(2)}) collective-permute-start(f32[16,16384]{1,0:T(8,128)S(1)} %fusion.23), channel_id=1, source_target_pairs={{0,64},{64,128},{128,192},{192,256},{256,320},{320,384},{384,448},... | collective-permute-start | bytes 3145736 | tf_op jit(solution)/shard_map/while/body/eval_jaxpr/ppermute | solution.py:10
  307.6 23.9 %collective-permute-start.1 = (f32[16]{0:T(128)S(1)}, f32[16]{0:T(128)S(1)}, u32[]{:S(2)}, u32[]{:S(2)}) collective-permute-start(f32[16]{0:T(128)S(1)} %get-tuple-element.336), channel_id=1, source_target_pairs={{0,64},{64,128},{128,192},{192,256},{256,320},{320,384},{384,448},... | collective-permute-start | bytes 200 | tf_op jit(solution)/shard_map/while/body/eval_jaxpr/ppermute | solution.py:10
  339.5 0.8 copy-start
  341.3 24.8 %collective-permute-start = (f32[16,16384]{1,0:T(8,128)S(1)}, f32[16,16384]{1,0:T(8,128)S(1)}, u32[]{:S(2)}, u32[]{:S(2)}) collective-permute-start(f32[16,16384]{1,0:T(8,128)S(1)} %fusion.23), channel_id=1, source_target_pairs={{0,64},{64,128},{128,192},{192,256},{256,320},{320,384},{384,448},... | collective-permute-start | bytes 3145736 | tf_op jit(solution)/shard_map/while/body/eval_jaxpr/ppermute | solution.py:10
  343.2 22.9 %collective-permute-start.1 = (f32[16]{0:T(128)S(1)}, f32[16]{0:T(128)S(1)}, u32[]{:S(2)}, u32[]{:S(2)}) collective-permute-start(f32[16]{0:T(128)S(1)} %get-tuple-element.336), channel_id=1, source_target_pairs={{0,64},{64,128},{128,192},{192,256},{256,320},{320,384},{384,448},... | collective-permute-start | bytes 200 | tf_op jit(solution)/shard_map/while/body/eval_jaxpr/ppermute | solution.py:10
  374.1 0.8 copy-start
  375.9 23.8 %collective-permute-start = (f32[16,16384]{1,0:T(8,128)S(1)}, f32[16,16384]{1,0:T(8,128)S(1)}, u32[]{:S(2)}, u32[]{:S(2)}) collective-permute-start(f32[16,16384]{1,0:T(8,128)S(1)} %fusion.23), channel_id=1, source_target_pairs={{0,64},{64,128},{128,192},{192,256},{256,320},{320,384},{384,448},... | collective-permute-start | bytes 3145736 | tf_op jit(solution)/shard_map/while/body/eval_jaxpr/ppermute | solution.py:10
  377.8 21.9 %collective-permute-start.1 = (f32[16]{0:T(128)S(1)}, f32[16]{0:T(128)S(1)}, u32[]{:S(2)}, u32[]{:S(2)}) collective-permute-start(f32[16]{0:T(128)S(1)} %get-tuple-element.336), channel_id=1, source_target_pairs={{0,64},{64,128},{128,192},{192,256},{256,320},{320,384},{384,448},... | collective-permute-start | bytes 200 | tf_op jit(solution)/shard_map/while/body/eval_jaxpr/ppermute | solution.py:10
  407.7 0.8 copy-start
  409.5 22.8 %collective-permute-start = (f32[16,16384]{1,0:T(8,128)S(1)}, f32[16,16384]{1,0:T(8,128)S(1)}, u32[]{:S(2)}, u32[]{:S(2)}) collective-permute-start(f32[16,16384]{1,0:T(8,128)S(1)} %fusion.23), channel_id=1, source_target_pairs={{0,64},{64,128},{128,192},{192,256},{256,320},{320,384},{384,448},... | collective-permute-start | bytes 3145736 | tf_op jit(solution)/shard_map/while/body/eval_jaxpr/ppermute | solution.py:10
  411.4 20.9 %collective-permute-start.1 = (f32[16]{0:T(128)S(1)}, f32[16]{0:T(128)S(1)}, u32[]{:S(2)}, u32[]{:S(2)}) collective-permute-start(f32[16]{0:T(128)S(1)} %get-tuple-element.336), channel_id=1, source_target_pairs={{0,64},{64,128},{128,192},{192,256},{256,320},{320,384},{384,448},... | collective-permute-start | bytes 200 | tf_op jit(solution)/shard_map/while/body/eval_jaxpr/ppermute | solution.py:10
  432.3 0.5 copy-start.1
  432.3 0.5 copy-start.2
Sparse Core Ops, SparseCore 0:
  10.1 133.4 all-gather.1
where the time goes:
time: 441 us; the launch traced here: 440 us
  waiting for transfers between devices  275 us (62%)
  starting transfers between devices  66 us (15%)
  matrix products  52.6 us (12%)
  other arithmetic  21.2 us (5%)
  between operations  14.1 us (3%)
  local copies, waits for them, and re-layouts  10 us (2%)
    ppermute x16, waiting for transfers between devices, passed_along(): lax.ppermute(value, axis, [(source, source + steps) for source in range(f...  144 us
    all_gather x1, waiting for transfers between devices, body(): whole = lax.all_gather(tensors, 'blk', axis=2, tiled=True)[0]  131 us
    ppermute x16, starting transfers between devices, passed_along(): lax.ppermute(value, axis, [(source, source + steps) for source in range(f...  66 us
    dot_general x8, matrix products, site_images(): jnp.einsum('rck,bckl->brcl', blocks, weights, preferred_element_type=jnp....  51.7 us
    while x8, other arithmetic  10.6 us
  transfers between devices with their start and end apart: 17, of which 9 were waited for; matrix products, arithmetic and copies ran while one was open for 1% of the time, Pallas kernels for 0%

commit v1 on v0

--- a/solution.py
+++ b/solution.py
@@ -67,13 +67,19 @@
 
 
 def body(bits, labels, left, tensors):
+
+    def _see_unit(panel, along_dim):
+        return jnp.concatenate(
+            lax.all_to_all(jnp.stack(lax.psum(1, "blk") * [panel]), "blk", 0, 0), axis=along_dim
+        )
+
     block = tensors.shape[-1]
     count_blocks = labels.shape[0]
     width = count_blocks * block
     rows = bits.shape[1]
     ordered = charge_order(labels, left, block)
     count = 1
-    whole = lax.all_gather(tensors, "blk", axis=2, tiled=True)[0]
+    whole = _see_unit(tensors, 2)[0]
 
     def advance(state, bit_rows):
         image = site_images(state, whole, block)

time: 441 us -> 691 us (1.57)
  the two profiles are of different devices: /device:TPU:2 before, /device:TPU:46 now
where the time goes in v1:
time: 691 us; the launch traced here: 690 us
  waiting for transfers between devices  542 us (78%)
  matrix products  51.9 us (8%)
  starting transfers between devices  51.8 us (7%)
  other arithmetic  29.9 us (4%)
  local copies, waits for them, and re-layouts  13.6 us (2%)
    all_to_all x1, waiting for transfers between devices, _see_unit(): lax.all_to_all(jnp.stack(lax.psum(1, 'blk') * [panel]), 'blk', 0, 0)  367 us
    ppermute x16, waiting for transfers between devices, passed_along(): lax.ppermute(value, axis, [(source, source + steps) for source in range(f...  174 us
    dot_general x8, matrix products, site_images(): jnp.einsum('rck,bckl->brcl', blocks, weights, preferred_element_type=jnp....  51.6 us
    ppermute x16, starting transfers between devices, passed_along(): lax.ppermute(value, axis, [(source, source + steps) for source in range(f...  34.8 us
    all_to_all x1, starting transfers between devices, _see_unit(): lax.all_to_all(jnp.stack(lax.psum(1, 'blk') * [panel]), 'blk', 0, 0)  17 us
  transfers between devices with their start and end apart: 17, of which 9 were waited for; matrix products, arithmetic and copies ran while one was open for 0% of the time, Pallas kernels for 0%

profile of v1, /device:TPU:46, one launch (start us, length us, event | category | flops | bytes accessed | tf_op | source)
XLA Modules:
  0.0 690.0 jit_solution(10885809408844647569)
XLA Ops:
  0.6 0.9 copy.15
  1.5 5.3 stack.2
  6.9 17.0 %all-to-all-start = ((bf16[64,1,2,2,128,128]{5,4,2,3,1,0:T(8,128)(2,1)}), bf16[64,1,2,2,128,128]{5,4,2,3,1,0:T(8,128)(2,1)}, u32[]{:S(2)}, u32[]{:S(2)}) async-start(bf16[64,1,2,2,128,128]{5,4,2,3,1,0:T(8,128)(2,1)} %stack.2), calls=%async_computation | async-start | bytes 16777216 | tf_op jit(solution)/shard_map/all_to_all | solution.py:73
  24.3 0.6 copy.29
  24.9 1.2 reshape.97
  26.1 367.3 %all-to-all-done = bf16[64,1,2,2,128,128]{5,4,2,3,1,0:T(8,128)(2,1)} async-done(((bf16[64,1,2,2,128,128]{5,4,2,3,1,0:T(8,128)(2,1)}), bf16[64,1,2,2,128,128]{5,4,2,3,1,0:T(8,128)(2,1)}, u32[]{:S(2)}, u32[]{:S(2)}) %all-to-all-start) | async-done | bytes 8388640 | tf_op jit(solution)/shard_map/all_to_all | solution.py:73
  393.3 296.1 %while.21 = (s32[]{:T(128)}, f32[16,16384]{1,0:T(8,128)S(1)}, f32[16]{0:T(128)S(1)}, f32[1,16]{1,0:T(1,128)S(1)}, f32[1,16]{1,0:T(1,128)S(1)}, /*index=5*/s32[1,...) while((s32[]{:T(128)}, f32[16,16384]{1,0:T(8,128)S(1)}, ...), condition=%wide.region_3.4_spmd.clone, body=%wide.region_0.3_spmd.clone.sunk | while | flops 807403776 | bytes 34604624 | solution.py:65
  393.3 1.3 fusion.21
  394.9 6.4 convolution_bitcast_fusion.2
  401.3 0.4 multiply_reduce_fusion.4
  402.5 1.7 fusion.23
  404.2 4.2 collective-permute-start
  408.4 1.9 collective-permute-start.1
  410.3 23.4 %collective-permute-done.1 = f32[16]{0:T(128)S(1)} collective-permute-done((f32[16]{0:T(128)S(1)}, f32[16]{0:T(128)S(1)}, u32[]{:S(2)}, u32[]{:S(2)}) %collective-permute-start.1) | collective-permute-done | bytes 96 | tf_op jit(solution)/shard_map/while/body/eval_jaxpr/ppermute | solution.py:10
  433.8 1.3 fusion.21
  435.3 6.4 convolution_bitcast_fusion.2
  441.8 0.4 multiply_reduce_fusion.4
  442.9 1.7 fusion.23
  444.6 3.3 collective-permute-start
  447.9 1.9 collective-permute-start.1
  449.9 23.4 %collective-permute-done.1 = f32[16]{0:T(128)S(1)} collective-permute-done((f32[16]{0:T(128)S(1)}, f32[16]{0:T(128)S(1)}, u32[]{:S(2)}, u32[]{:S(2)}) %collective-permute-start.1) | collective-permute-done | bytes 96 | tf_op jit(solution)/shard_map/while/body/eval_jaxpr/ppermute | solution.py:10
  473.3 1.3 fusion.21
  474.8 6.4 convolution_bitcast_fusion.2
  481.3 0.4 multiply_reduce_fusion.4
  482.4 1.7 fusion.23
  484.1 2.4 collective-permute-start
  486.5 1.9 collective-permute-start.1
  488.4 23.3 %collective-permute-done.1 = f32[16]{0:T(128)S(1)} collective-permute-done((f32[16]{0:T(128)S(1)}, f32[16]{0:T(128)S(1)}, u32[]{:S(2)}, u32[]{:S(2)}) %collective-permute-start.1) | collective-permute-done | bytes 96 | tf_op jit(solution)/shard_map/while/body/eval_jaxpr/ppermute | solution.py:10
  511.8 1.3 fusion.21
  513.3 6.4 convolution_bitcast_fusion.2
  519.8 0.4 multiply_reduce_fusion.4
  520.9 1.7 fusion.23
  522.6 1.9 collective-permute-start
  524.5 1.9 collective-permute-start.1
  526.5 22.8 %collective-permute-done.1 = f32[16]{0:T(128)S(1)} collective-permute-done((f32[16]{0:T(128)S(1)}, f32[16]{0:T(128)S(1)}, u32[]{:S(2)}, u32[]{:S(2)}) %collective-permute-start.1) | collective-permute-done | bytes 96 | tf_op jit(solution)/shard_map/while/body/eval_jaxpr/ppermute | solution.py:10
  549.3 1.3 fusion.21
  550.8 6.4 convolution_bitcast_fusion.2
  557.3 0.4 multiply_reduce_fusion.4
  558.4 1.7 fusion.23
  560.1 1.9 collective-permute-start
  562.0 1.9 collective-permute-start.1
  564.0 21.8 %collective-permute-done.1 = f32[16]{0:T(128)S(1)} collective-permute-done((f32[16]{0:T(128)S(1)}, f32[16]{0:T(128)S(1)}, u32[]{:S(2)}, u32[]{:S(2)}) %collective-permute-start.1) | collective-permute-done | bytes 96 | tf_op jit(solution)/shard_map/while/body/eval_jaxpr/ppermute | solution.py:10
  585.8 1.3 fusion.21
  587.3 6.4 convolution_bitcast_fusion.2
  593.8 0.4 multiply_reduce_fusion.4
  594.9 1.7 fusion.23
  596.6 1.9 collective-permute-start
  598.6 1.9 collective-permute-start.1
  600.5 20.8 %collective-permute-done.1 = f32[16]{0:T(128)S(1)} collective-permute-done((f32[16]{0:T(128)S(1)}, f32[16]{0:T(128)S(1)}, u32[]{:S(2)}, u32[]{:S(2)}) %collective-permute-start.1) | collective-permute-done | bytes 96 | tf_op jit(solution)/shard_map/while/body/eval_jaxpr/ppermute | solution.py:10
  621.3 1.3 fusion.21
  622.9 6.4 convolution_bitcast_fusion.2
  629.3 0.4 multiply_reduce_fusion.4
  630.5 1.7 fusion.23
  632.2 1.9 collective-permute-start
  634.1 1.9 collective-permute-start.1
  636.0 19.8 %collective-permute-done.1 = f32[16]{0:T(128)S(1)} collective-permute-done((f32[16]{0:T(128)S(1)}, f32[16]{0:T(128)S(1)}, u32[]{:S(2)}, u32[]{:S(2)}) %collective-permute-start.1) | collective-permute-done | bytes 96 | tf_op jit(solution)/shard_map/while/body/eval_jaxpr/ppermute | solution.py:10
  655.9 1.3 fusion.21
  657.4 6.4 convolution_bitcast_fusion.2
  663.9 0.4 multiply_reduce_fusion.4
  665.0 1.7 fusion.23
  666.7 1.9 collective-permute-start
  668.6 1.9 collective-permute-start.1
  670.6 18.8 %collective-permute-done.1 = f32[16]{0:T(128)S(1)} collective-permute-done((f32[16]{0:T(128)S(1)}, f32[16]{0:T(128)S(1)}, u32[]{:S(2)}, u32[]{:S(2)}) %collective-permute-start.1) | collective-permute-done | bytes 96 | tf_op jit(solution)/shard_map/while/body/eval_jaxpr/ppermute | solution.py:10
  689.4 0.5 copy-done.2
  (86 shorter events, 7.9 us)
Async XLA Ops:
  6.9 17.0 %copy-start = (bf16[16,16384]{1,0:T(8,128)(2,1)S(1)}, bf16[16,16384]{1,0:T(8,128)(2,1)}, u32[]{:S(2)}) copy-start(bf16[16,16384]{1,0:T(8,128)(2,1)} %param.8) | copy-start | bytes 1572868
  6.9 17.1 %copy-start.4 = (s32[128]{0:T(128)S(1)}, s32[128]{0:T(128)}, u32[]{:S(2)}) copy-start(s32[128]{0:T(128)} %param.7) | copy-start | bytes 1540
  6.9 386.4 %copy-start.1 = (s32[1,16]{1,0:T(1,128)S(1)}, s32[1,16]{1,0:T(1,128)}, u32[]{:S(2)}) copy-start(s32[1,16]{1,0:T(1,128)} %param.6) | copy-start | bytes 196
  6.9 386.4 %all-to-all-start = ((bf16[64,1,2,2,128,128]{5,4,2,3,1,0:T(8,128)(2,1)}), bf16[64,1,2,2,128,128]{5,4,2,3,1,0:T(8,128)(2,1)}, u32[]{:S(2)}, u32[]{:S(2)}) async-start(bf16[64,1,2,2,128,128]{5,4,2,3,1,0:T(8,128)(2,1)} %stack.2), calls=%async_computation | async-start | bytes 16777216 | tf_op jit(solution)/shard_map/all_to_all | solution.py:73
  404.2 29.6 %collective-permute-start = (f32[16,16384]{1,0:T(8,128)}, f32[16,16384]{1,0:T(8,128)S(1)}, u32[]{:S(2)}, u32[]{:S(2)}) collective-permute-start(f32[16,16384]{1,0:T(8,128)} %fusion.23), channel_id=1, source_target_pairs={{0,64},{64,128},{128,192},{192,256},{256,320},{320,384},{384,448},... | collective-permute-start | bytes 3145736 | tf_op jit(solution)/shard_map/while/body/eval_jaxpr/ppermute | solution.py:10
  408.4 25.4 %collective-permute-start.1 = (f32[16]{0:T(128)S(1)}, f32[16]{0:T(128)S(1)}, u32[]{:S(2)}, u32[]{:S(2)}) collective-permute-start(f32[16]{0:T(128)S(1)} %get-tuple-element.336), channel_id=1, source_target_pairs={{0,64},{64,128},{128,192},{192,256},{256,320},{320,384},{384,448},... | collective-permute-start | bytes 200 | tf_op jit(solution)/shard_map/while/body/eval_jaxpr/ppermute | solution.py:10
  444.6 28.7 %collective-permute-start = (f32[16,16384]{1,0:T(8,128)}, f32[16,16384]{1,0:T(8,128)S(1)}, u32[]{:S(2)}, u32[]{:S(2)}) collective-permute-start(f32[16,16384]{1,0:T(8,128)} %fusion.23), channel_id=1, source_target_pairs={{0,64},{64,128},{128,192},{192,256},{256,320},{320,384},{384,448},... | collective-permute-start | bytes 3145736 | tf_op jit(solution)/shard_map/while/body/eval_jaxpr/ppermute | solution.py:10
  447.9 25.3 %collective-permute-start.1 = (f32[16]{0:T(128)S(1)}, f32[16]{0:T(128)S(1)}, u32[]{:S(2)}, u32[]{:S(2)}) collective-permute-start(f32[16]{0:T(128)S(1)} %get-tuple-element.336), channel_id=1, source_target_pairs={{0,64},{64,128},{128,192},{192,256},{256,320},{320,384},{384,448},... | collective-permute-start | bytes 200 | tf_op jit(solution)/shard_map/while/body/eval_jaxpr/ppermute | solution.py:10
  484.1 27.7 %collective-permute-start = (f32[16,16384]{1,0:T(8,128)}, f32[16,16384]{1,0:T(8,128)S(1)}, u32[]{:S(2)}, u32[]{:S(2)}) collective-permute-start(f32[16,16384]{1,0:T(8,128)} %fusion.23), channel_id=1, source_target_pairs={{0,64},{64,128},{128,192},{192,256},{256,320},{320,384},{384,448},... | collective-permute-start | bytes 3145736 | tf_op jit(solution)/shard_map/while/body/eval_jaxpr/ppermute | solution.py:10
  486.5 25.3 %collective-permute-start.1 = (f32[16]{0:T(128)S(1)}, f32[16]{0:T(128)S(1)}, u32[]{:S(2)}, u32[]{:S(2)}) collective-permute-start(f32[16]{0:T(128)S(1)} %get-tuple-element.336), channel_id=1, source_target_pairs={{0,64},{64,128},{128,192},{192,256},{256,320},{320,384},{384,448},... | collective-permute-start | bytes 200 | tf_op jit(solution)/shard_map/while/body/eval_jaxpr/ppermute | solution.py:10
  522.6 26.7 %collective-permute-start = (f32[16,16384]{1,0:T(8,128)}, f32[16,16384]{1,0:T(8,128)S(1)}, u32[]{:S(2)}, u32[]{:S(2)}) collective-permute-start(f32[16,16384]{1,0:T(8,128)} %fusion.23), channel_id=1, source_target_pairs={{0,64},{64,128},{128,192},{192,256},{256,320},{320,384},{384,448},... | collective-permute-start | bytes 3145736 | tf_op jit(solution)/shard_map/while/body/eval_jaxpr/ppermute | solution.py:10
  524.5 24.8 %collective-permute-start.1 = (f32[16]{0:T(128)S(1)}, f32[16]{0:T(128)S(1)}, u32[]{:S(2)}, u32[]{:S(2)}) collective-permute-start(f32[16]{0:T(128)S(1)} %get-tuple-element.336), channel_id=1, source_target_pairs={{0,64},{64,128},{128,192},{192,256},{256,320},{320,384},{384,448},... | collective-permute-start | bytes 200 | tf_op jit(solution)/shard_map/while/body/eval_jaxpr/ppermute | solution.py:10
  560.1 25.7 %collective-permute-start = (f32[16,16384]{1,0:T(8,128)}, f32[16,16384]{1,0:T(8,128)S(1)}, u32[]{:S(2)}, u32[]{:S(2)}) collective-permute-start(f32[16,16384]{1,0:T(8,128)} %fusion.23), channel_id=1, source_target_pairs={{0,64},{64,128},{128,192},{192,256},{256,320},{320,384},{384,448},... | collective-permute-start | bytes 3145736 | tf_op jit(solution)/shard_map/while/body/eval_jaxpr/ppermute | solution.py:10
  562.0 23.8 %collective-permute-start.1 = (f32[16]{0:T(128)S(1)}, f32[16]{0:T(128)S(1)}, u32[]{:S(2)}, u32[]{:S(2)}) collective-permute-start(f32[16]{0:T(128)S(1)} %get-tuple-element.336), channel_id=1, source_target_pairs={{0,64},{64,128},{128,192},{192,256},{256,320},{320,384},{384,448},... | collective-permute-start | bytes 200 | tf_op jit(solution)/shard_map/while/body/eval_jaxpr/ppermute | solution.py:10
  596.6 24.7 %collective-permute-start = (f32[16,16384]{1,0:T(8,128)}, f32[16,16384]{1,0:T(8,128)S(1)}, u32[]{:S(2)}, u32[]{:S(2)}) collective-permute-start(f32[16,16384]{1,0:T(8,128)} %fusion.23), channel_id=1, source_target_pairs={{0,64},{64,128},{128,192},{192,256},{256,320},{320,384},{384,448},... | collective-permute-start | bytes 3145736 | tf_op jit(solution)/shard_map/while/body/eval_jaxpr/ppermute | solution.py:10
  598.6 22.8 %collective-permute-start.1 = (f32[16]{0:T(128)S(1)}, f32[16]{0:T(128)S(1)}, u32[]{:S(2)}, u32[]{:S(2)}) collective-permute-start(f32[16]{0:T(128)S(1)} %get-tuple-element.336), channel_id=1, source_target_pairs={{0,64},{64,128},{128,192},{192,256},{256,320},{320,384},{384,448},... | collective-permute-start | bytes 200 | tf_op jit(solution)/shard_map/while/body/eval_jaxpr/ppermute | solution.py:10
  632.2 23.7 %collective-permute-start = (f32[16,16384]{1,0:T(8,128)}, f32[16,16384]{1,0:T(8,128)S(1)}, u32[]{:S(2)}, u32[]{:S(2)}) collective-permute-start(f32[16,16384]{1,0:T(8,128)} %fusion.23), channel_id=1, source_target_pairs={{0,64},{64,128},{128,192},{192,256},{256,320},{320,384},{384,448},... | collective-permute-start | bytes 3145736 | tf_op jit(solution)/shard_map/while/body/eval_jaxpr/ppermute | solution.py:10
  634.1 21.8 %collective-permute-start.1 = (f32[16]{0:T(128)S(1)}, f32[16]{0:T(128)S(1)}, u32[]{:S(2)}, u32[]{:S(2)}) collective-permute-start(f32[16]{0:T(128)S(1)} %get-tuple-element.336), channel_id=1, source_target_pairs={{0,64},{64,128},{128,192},{192,256},{256,320},{320,384},{384,448},... | collective-permute-start | bytes 200 | tf_op jit(solution)/shard_map/while/body/eval_jaxpr/ppermute | solution.py:10
  666.7 22.7 %collective-permute-start = (f32[16,16384]{1,0:T(8,128)}, f32[16,16384]{1,0:T(8,128)S(1)}, u32[]{:S(2)}, u32[]{:S(2)}) collective-permute-start(f32[16,16384]{1,0:T(8,128)} %fusion.23), channel_id=1, source_target_pairs={{0,64},{64,128},{128,192},{192,256},{256,320},{320,384},{384,448},... | collective-permute-start | bytes 3145736 | tf_op jit(solution)/shard_map/while/body/eval_jaxpr/ppermute | solution.py:10
  668.6 20.8 %collective-permute-start.1 = (f32[16]{0:T(128)S(1)}, f32[16]{0:T(128)S(1)}, u32[]{:S(2)}, u32[]{:S(2)}) collective-permute-start(f32[16]{0:T(128)S(1)} %get-tuple-element.336), channel_id=1, source_target_pairs={{0,64},{64,128},{128,192},{192,256},{256,320},{320,384},{384,448},... | collective-permute-start | bytes 200 | tf_op jit(solution)/shard_map/while/body/eval_jaxpr/ppermute | solution.py:10
  689.4 0.5 copy-start.2
  689.4 0.5 copy-start.3
